TPU v7x, 32 devices: a whole 2x2x4 slice. The times are simulated.
32 devices in a mesh: section: 4 (over y, core), site: 8 (over z, x).
Axes of the slice: x: 2, y: 2, z: 4, core: 2. Of those that a mesh axis runs over, the one named last changes fastest.
Arguments:
- acts: bfloat16 [4, 8, 4096], P('section', 'site'), may hold values from -36 to 36
- patches: bfloat16 [4, 2048, 1024], P('section', 'site'), may hold values from -36 to 36
- site_tiles: int32 [8, 256], replicated, may hold values from 0 to 2047, as said below
- site_count: int32 [8], replicated, may hold values from 128 to 256, as said below
- q_weight: bfloat16 [4, 2048, 4096], P('section', 'site'), may hold values from -0.09375 to 0.09375
- q_gain: float32 [4, 128], P('section'), may hold values from 1 to 2.5
- k_gain: float32 [4, 128], P('section'), may hold values from 1 to 2.5
- tile_in: bfloat16 [4, 1024, 512], P('section', 'site'), may hold values from -0.1875 to 0.1875
- tile_out: bfloat16 [4, 512, 4096], P('section', 'site'), may hold values from -0.25 to 0.25
- out_weight: bfloat16 [4, 2048, 4096], P('section', 'site'), may hold values from -0.125 to 0.125
- ffn_gain: float32 [4, 4096], P('section'), may hold values from 0.25 to 1.75
- gate_weight: bfloat16 [4, 7168, 4096], P('section', 'site'), may hold values from -0.09375 to 0.09375
- up_weight: bfloat16 [4, 7168, 4096], P('section', 'site'), may hold values from -0.09375 to 0.09375
- down_weight: bfloat16 [4, 7168, 4096], P('section', 'site'), may hold values from -0.0625 to 0.0625
Outputs:
- passed: bfloat16 [4, 8, 4096], P('section', 'site')
Inputs may be any that keep to these rules, and one draw needn't show every extreme that they name: `site_tiles`: shard k owns tiles k * 256 to (k + 1) * 256 - 1. Of the live entries (l < site_count[n]) of the one site held by a device, at most 40 name tiles of one shard, and in every device exactly 40 name tiles of some shard. All entries of one device's sites are different tiles. `site_count`: sites n with n % 1 == 0, except site 8 - 1, have all 256 entries live; site 8 - 1 has exactly 128.
All inputs are finite; a program needn't handle non-finite values.
Results may differ from a plain program's by a relative error of at most 0.0055.
Values may be sent and summed in bfloat16 or wider, within the bound.
No kernel may reach another device: no remote copies, remote signals or barrier semaphores. Data moves between devices by JAX's collectives and lax.ppermute only.
A program may use at most 128 MiB of HBM per device.

v0:
```python
import math
import jax
import jax.numpy as jnp
from jax import lax
from jax.sharding import PartitionSpec as P

HEADS = 16
epsilon = 1e-05


def shifted(value, axis, steps):
    count = lax.axis_size(axis)
    pairs = [(source, (source + steps) % count) for source in range(count)]
    return lax.ppermute(value, axis, pairs)


def by_rows(left, weight_rows):
    return lax.dot_general(
        left, weight_rows, (((1,), (1,)), ((), ())), preferred_element_type=jnp.float32
    )


def head_norm(values, gain_row):
    shaped = values.astype(jnp.float32).reshape(values.shape[0], -1, gain_row.shape[0])
    scaled = (
        shaped * lax.rsqrt(jnp.mean(shaped * shaped, axis=-1, keepdims=True) + epsilon) * gain_row
    )
    return scaled.reshape(values.shape[0], -1)


def rms_norm(values, gain_row):
    return (
        values * lax.rsqrt(jnp.mean(values * values, axis=-1, keepdims=True) + epsilon) * gain_row
    )


def encode(tile_rows, weight_in, weight_out, key_gain):
    hidden = jax.nn.gelu(
        jnp.dot(tile_rows, weight_in, preferred_element_type=jnp.float32), approximate=True
    ).astype(jnp.bfloat16)
    keyval = jnp.dot(hidden, weight_out, preferred_element_type=jnp.float32)
    half_width = keyval.shape[1] // 2
    normed_keys = head_norm(keyval[:, :half_width], key_gain)
    return jnp.concatenate([normed_keys, keyval[:, half_width:]], axis=1).astype(jnp.bfloat16)


def shards(
    acts,
    patches,
    site_tiles,
    site_count,
    q_weight,
    q_gain,
    k_gain,
    tile_in,
    tile_out,
    out_weight,
    ffn_gain,
    gate_weight,
    up_weight,
    down_weight,
):
    group_size = lax.axis_size("site")
    my_index = lax.axis_index("site")
    sites_here = acts.shape[1]
    list_width = site_tiles.shape[1]
    tiles_here = patches.shape[1]
    head_size = q_gain.shape[1]
    capacity = max(2, 5 * sites_here * list_width // (4 * group_size))
    current = acts[0]
    weight_in, weight_out = (
        lax.all_gather(tile_in[0], "site", axis=0, tiled=True),
        lax.all_gather(tile_out[0], "site", axis=0, tiled=True),
    )
    slot_index = jnp.arange(list_width, dtype=jnp.int32)
    live_all = slot_index[None, :] < site_count[:, None]
    owner_all = site_tiles // tiles_here
    local_all = site_tiles % tiles_here
    mine_mask = jnp.logical_and(live_all, owner_all == my_index).astype(jnp.int32)
    slot_rank = jnp.cumsum(mine_mask, axis=1) - 1
    targets = jnp.where(
        mine_mask == 1,
        jnp.arange(group_size, dtype=jnp.int32)[:, None] * capacity + slot_rank,
        group_size * capacity,
    )
    send_index = (
        jnp.zeros((group_size * capacity + 1,), jnp.int32)
        .at[targets.reshape(-1)]
        .set(local_all.reshape(-1))
    )
    send_index = send_index[:-1].reshape(group_size, capacity)
    my_tiles = lax.dynamic_slice_in_dim(site_tiles, my_index * sites_here, sites_here, 0)
    my_count = lax.dynamic_slice_in_dim(site_count, my_index * sites_here, sites_here, 0)
    my_live = slot_index[None, :] < my_count[:, None]
    my_owner = (my_tiles // tiles_here).reshape(-1)
    one_hot = jnp.logical_and(
        my_owner[:, None] == jnp.arange(group_size, dtype=jnp.int32)[None, :],
        my_live.reshape(-1)[:, None],
    ).astype(jnp.int32)
    my_rank = jnp.sum(jnp.cumsum(one_hot, axis=0) * one_hot, axis=1) - 1
    fetch_index = jnp.where(my_live.reshape(-1), my_owner * capacity + my_rank, 0)
    encoded = encode(patches[0], weight_in, weight_out, k_gain[0])
    arrived = lax.all_to_all(encoded[send_index], "site", split_axis=0, concat_axis=0, tiled=True)
    pair_kv = arrived.reshape(group_size * capacity, -1)[fetch_index]
    pair_kv = pair_kv.reshape(sites_here, list_width, 2, HEADS, head_size)
    everyone = lax.all_gather(current, "site", axis=0, tiled=True)
    q_part = by_rows(everyone, q_weight[0]).astype(jnp.bfloat16)
    my_queries = lax.all_to_all(q_part, "site", split_axis=0, concat_axis=1, tiled=True)
    queries = head_norm(my_queries, q_gain[0]).astype(jnp.bfloat16)
    query_heads = queries.reshape(sites_here, HEADS, head_size)
    scores = jnp.einsum(
        "nhd,nlhd->nhl", query_heads, pair_kv[:, :, 0], preferred_element_type=jnp.float32
    ) / math.sqrt(head_size)
    exponents = jnp.exp(scores) * my_live.astype(jnp.float32)[:, None, :]
    weights = (exponents / jnp.sum(exponents, axis=-1, keepdims=True)).astype(jnp.bfloat16)
    combined = jnp.einsum(
        "nhl,nlhd->nhd", weights, pair_kv[:, :, 1], preferred_element_type=jnp.float32
    )
    combined = combined.reshape(sites_here, -1).astype(jnp.bfloat16)
    columns = lax.all_to_all(combined, "site", split_axis=1, concat_axis=0, tiled=True)
    residual = current.astype(jnp.float32) + lax.psum_scatter(
        jnp.dot(columns, out_weight[0], preferred_element_type=jnp.float32),
        "site",
        scatter_dimension=0,
        tiled=True,
    )
    normed = rms_norm(residual, ffn_gain[0]).astype(jnp.bfloat16)
    normed_rows = lax.all_gather(normed, "site", axis=0, tiled=True)
    gate_sum = by_rows(normed_rows, gate_weight[0])
    up_sum = by_rows(normed_rows, up_weight[0])
    hidden = (jax.nn.silu(gate_sum) * up_sum).astype(jnp.bfloat16)
    output_rows = (
        residual
        + lax.psum_scatter(
            jnp.dot(hidden, down_weight[0], preferred_element_type=jnp.float32),
            "site",
            scatter_dimension=0,
            tiled=True,
        )
    ).astype(jnp.bfloat16)
    return shifted(output_rows[None], "section", 1)


def solution(mesh):
    return jax.shard_map(
        shards,
        mesh=mesh,
        in_specs=(
            P("section", "site", None),
            P("section", "site", None),
            P(),
            P(),
            P("section", "site", None),
            P("section", None),
            P("section", None),
            P("section", "site", None),
            P("section", "site", None),
            P("section", "site", None),
            P("section", None),
            P("section", "site", None),
            P("section", "site", None),
            P("section", "site", None),
        ),
        out_specs=P("section", "site", None),
        check_vma=False,
    )
```

profile of v0, /device:TPU:0, one launch (start us, length us, event | category | flops | bytes accessed | tf_op | source)
XLA Modules:
  0.0 436.5 jit_solution(14200362407360964330)
XLA Ops:
  6.6 0.7 all-gather.7.cloned.1.call-update
  7.3 0.7 all-gather.9.cloned.1.call-update
  8.0 32.7 %all-gather = bf16[8,1,4096]{2,1,0:T(2,128)(2,1)S(1)} all-gather(bf16[1,1,4096]{2,1,0:T(2,128)(2,1)} %param.14), channel_id=2, replica_groups=mesh['section'=4,'site'=8] {'site'}, dimensions={0}, use_global_device_ids=true | all-gather | bytes 73728 | tf_op jit(solution)/shard_map/all_gather | solution.py:106
  40.7 2.2 fusion.23
  43.0 0.6 broadcast.242
  43.6 0.6 reduce.9
  44.2 0.6 reshape.383
  44.8 5.4 %all-to-all-start = ((bf16[8,2,128]{2,1,0:T(2,128)(2,1)}), bf16[8,2,128]{2,1,0:T(2,128)(2,1)S(1)}, u32[]{:S(2)}, u32[]{:S(2)}) async-start(bf16[8,2,128]{2,1,0:T(2,128)(2,1)} %reshape.383), calls=%async_computation | async-start | bytes 8192 | tf_op jit(solution)/shard_map/all_to_all | solution.py:108
  50.3 0.6 reduce-window.14
  50.9 0.2 slice_reduce_fusion.1
  51.3 8.0 %scatter_custom_fusion = s32[321]{0:T(512)S(1)} fusion(s32[2048]{0:T(1024)S(1)} %bitcast.159, s32[2048]{0:T(1024)S(1)} %bitcast.158, s32[]{:T(128)} %constant.85.clone.1), kind=kCustom, calls=%fused_computation.118 | custom fusion | bytes 1288 | tf_op jit(solution)/shard_map/scatter | solution.py:89
  59.6 67.3 %all-gather.9.cloned.1.call-done = bf16[1,512,4096]{2,1,0:T(8,128)(2,1)} async-done(((bf16[1,64,4096]{2,1,0:T(8,128)(2,1)}), bf16[1,512,4096]{2,1,0:T(8,128)(2,1)}) %all-gather.9.cloned.1.call-update) | async-done | bytes 4194320 | tf_op jit(solution)/shard_map/all_gather | solution.py:73
  126.9 6.1 %fusion.6 = f32[256,4096]{1,0:T(8,128)} fusion(bf16[1,512,4096]{2,1,0:T(8,128)(2,1)} %all-gather.9.cloned.1.call-done, bf16[1,1024,512]{2,1,0:T(8,128)(2,1)} %all-gather.7.cloned.1.call-done, bf16[1,256,1024]{2,1,0:T(8,128)(2,1)S(1)} %copy-done.1), kind=kOutput, calls=%fused_computation.9 | convolution fusion | flops 1343356928 | bytes 9961472 | tf_op jit(solution)/shard_map/dot_general | solution.py:41
  133.0 1.7 slice.54
  134.7 1.7 multiply_bitcast_fusion
  136.5 1.7 copy.37
  138.2 2.2 reduce_sum.46
  140.6 0.6 mul.170
  141.2 2.4 fusion.9
  143.6 1.5 pad_maximum_fusion
  145.1 9.9 %gather_fusion = bf16[320,4096]{1,0:T(8,128)(2,1)} fusion(bf16[256,4096]{1,0:T(8,128)(2,1)} %pad_maximum_fusion, s32[1024]{0:T(1024)S(1)} %pad_clamp_fusion.1), kind=kCustom, calls=%fused_computation | custom fusion | bytes 5244160 | tf_op jit(solution)/shard_map/gather | solution.py:103
  155.1 4.5 %all-to-all-start.1 = ((bf16[8,40,4096]{2,1,0:T(8,128)(2,1)}), bf16[8,40,4096]{2,1,0:T(8,128)(2,1)}, u32[]{:S(2)}, u32[]{:S(2)}) async-start(bf16[8,40,4096]{2,1,0:T(8,128)(2,1)} %bitcast.144), calls=%async_computation.1 | async-start | bytes 5242880 | tf_op jit(solution)/shard_map/all_to_all | solution.py:103
  159.6 0.2 all-reduce.5.cloned.1.call-start
  159.8 0.6 dynamic_slice.6
  160.4 0.7 add_compare_fusion
  161.1 0.6 reduce-window.16
  161.7 0.2 slice_reduce_fusion
  162.0 0.7 iota_compare_fusion.3
  162.7 0.7 compare_select_fusion.2
  163.7 54.5 %all-to-all-done.1 = bf16[8,40,4096]{2,1,0:T(8,128)(2,1)} async-done(((bf16[8,40,4096]{2,1,0:T(8,128)(2,1)}), bf16[8,40,4096]{2,1,0:T(8,128)(2,1)}, u32[]{:S(2)}, u32[]{:S(2)}) %all-to-all-start.1) | async-done | bytes 2621472 | tf_op jit(solution)/shard_map/all_to_all | solution.py:103
  218.2 7.3 %gather_fusion.1 = bf16[256,4096]{1,0:T(8,128)(2,1)} fusion(bf16[320,4096]{1,0:T(8,128)(2,1)} %bitcast.16, s32[1024]{0:T(1024)S(1)} %pad_clamp_fusion), kind=kCustom, calls=%fused_computation.1 | custom fusion | bytes 4195328 | tf_op jit(solution)/shard_map/gather | solution.py:104
  225.5 2.1 copy.41
  227.5 0.4 slice_bitcast_fusion.1
  227.9 0.4 fusion.30
  228.5 0.3 fusion.28
  228.9 0.7 reduce.10
  229.6 9.9 %all_to_all.31 = bf16[8,2,128]{2,1,0:T(2,128)(2,1)S(1)} all-to-all(bf16[8,2,128]{2,1,0:T(2,128)(2,1)S(1)} %reshape.385), channel_id=1, replica_groups=mesh['section'=4,'site'=8] {'site'}, dimensions={0} | all-to-all | bytes 8192 | tf_op jit(solution)/shard_map/all_to_all | solution.py:120
  239.4 1.0 fusion.10
  240.6 0.6 dynamic-slice
  241.2 66.5 %all-reduce.5.cloned.1.call-done = f32[8,4096]{1,0:T(8,128)} async-done(((f32[8,4096]{1,0:T(8,128)}), f32[8,4096]{1,0:T(8,128)}) %all-reduce.5.cloned.1.call-update) | async-done | bytes 131088
  307.6 2.2 multiply_reduce_fusion
  310.4 30.5 %all-gather.3 = bf16[8,1,4096]{2,1,0:T(2,128)(2,1)S(1)} all-gather(bf16[1,1,4096]{2,1,0:T(2,128)(2,1)S(1)} %convert_bitcast_fusion), channel_id=1, replica_groups=mesh['section'=4,'site'=8] {'site'}, dimensions={0}, use_global_device_ids=true | all-gather | bytes 73728 | tf_op jit(solution)/shard_map/all_gather | solution.py:128
  341.0 5.1 %fusion.4 = f32[8,896]{1,0:T(8,128)S(1)} fusion(bf16[1,896,4096]{2,1,0:T(8,128)(2,1)} %param.25, bf16[8,1,4096]{2,1,0:T(2,128)(2,1)S(1)} %all-gather.3), kind=kOutput, calls=%fused_computation.7 | convolution fusion | flops 58720256 | bytes 7434240 | tf_op jit(solution)/shard_map/dot_general | solution.py:18
  346.1 9.3 %fusion = f32[8,4096]{1,0:T(8,128)} fusion(bf16[1,896,4096]{2,1,0:T(8,128)(2,1)} %param.27, bf16[1,896,4096]{2,1,0:T(8,128)(2,1)} %param.26, f32[8,896]{1,0:T(8,128)S(1)} %fusion.4, bf16[8,1,4096]{2,1,0:T(2,128)(2,1)S(1)} %all-gather.3), kind=kOutput, calls=%fused_computation.3 | convolution fusion | flops 117483520 | bytes 14905344 | tf_op jit(solution)/shard_map/dot_general | solution.py:135
  355.4 69.1 %all-reduce.7.cloned.1.call-done = f32[8,4096]{1,0:T(8,128)} async-done(((f32[8,4096]{1,0:T(8,128)}), f32[8,4096]{1,0:T(8,128)}) %all-reduce.7.cloned.1.call-update) | async-done | bytes 131088
  424.6 1.6 fusion.68
  426.2 3.2 collective-permute-done
  429.4 0.6 copy.79
  (63 shorter events, 1.5 us)
Async XLA Ops:
  6.5 232.9 %copy-start = (bf16[1,256,4096]{2,1,0:T(8,128)(2,1)S(1)}, bf16[1,256,4096]{2,1,0:T(8,128)(2,1)}, u32[]{:S(2)}) copy-start(bf16[1,256,4096]{2,1,0:T(8,128)(2,1)} %param.23) | copy-start | bytes 6291460
  6.5 43.7 %copy-start.3 = (s32[8,256]{1,0:T(8,128)S(1)}, s32[8,256]{1,0:T(8,128)}, u32[]{:S(2)}) copy-start(s32[8,256]{1,0:T(8,128)} %param.16) | copy-start | bytes 24580
  6.5 43.7 %copy-start.6 = (s32[8]{0:T(128)S(1)}, s32[8]{0:T(128)}, u32[]{:S(2)}) copy-start(s32[8]{0:T(128)} %param.17) | copy-start | bytes 100
  6.5 53.0 %copy-start.5 = (f32[1,128]{1,0:T(1,128)S(1)}, f32[1,128]{1,0:T(1,128)}, u32[]{:S(2)}) copy-start(f32[1,128]{1,0:T(1,128)} %param.20) | copy-start | bytes 1540
  6.5 120.3 %copy-start.1 = (bf16[1,256,1024]{2,1,0:T(8,128)(2,1)S(1)}, bf16[1,256,1024]{2,1,0:T(8,128)(2,1)}, u32[]{:S(2)}) copy-start(bf16[1,256,1024]{2,1,0:T(8,128)(2,1)} %param.15) | copy-start | bytes 1572868
  6.5 53.0 %all-gather.7.cloned.1.call-start = ((), (), s32[]{:S(2)}) async-start(), calls=%async_computation.3 | async-start | bytes 1179648 | tf_op jit(solution)/shard_map/all_gather | solution.py:72
  7.3 119.6 %all-gather.9.cloned.1.call-start = ((), (), s32[]{:S(2)}) async-start(), calls=%async_computation.4 | async-start | bytes 4718592 | tf_op jit(solution)/shard_map/all_gather | solution.py:73
  44.8 110.3 %all-to-all-start = ((bf16[8,2,128]{2,1,0:T(2,128)(2,1)}), bf16[8,2,128]{2,1,0:T(2,128)(2,1)S(1)}, u32[]{:S(2)}, u32[]{:S(2)}) async-start(bf16[8,2,128]{2,1,0:T(2,128)(2,1)} %reshape.383), calls=%async_computation | async-start | bytes 8192 | tf_op jit(solution)/shard_map/all_to_all | solution.py:108
  155.1 8.5 %copy-start.7 = (f32[1,128]{1,0:T(1,128)S(1)}, f32[1,128]{1,0:T(1,128)}, u32[]{:S(2)}) copy-start(f32[1,128]{1,0:T(1,128)} %param.19) | copy-start | bytes 1540
  155.1 63.1 %all-to-all-start.1 = ((bf16[8,40,4096]{2,1,0:T(8,128)(2,1)}), bf16[8,40,4096]{2,1,0:T(8,128)(2,1)}, u32[]{:S(2)}, u32[]{:S(2)}) async-start(bf16[8,40,4096]{2,1,0:T(8,128)(2,1)} %bitcast.144), calls=%async_computation.1 | async-start | bytes 5242880 | tf_op jit(solution)/shard_map/all_to_all | solution.py:103
  159.6 148.0 %all-reduce.5.cloned.1.call-start = ((), (), s32[]{:S(2)}) async-start(), calls=%async_computation.5 | async-start | bytes 262144
  227.9 12.7 %copy-start.8 = (u32[32]{0:T(128)S(1)}, u32[32]{0:T(128)}, u32[]{:S(2)}) copy-start(u32[32]{0:T(128)} %constant.112) | copy-start | bytes 388
  227.9 79.7 %copy-start.2 = (bf16[1,1,4096]{2,1,0:T(2,128)(2,1)S(1)}, bf16[1,1,4096]{2,1,0:T(2,128)(2,1)}, u32[]{:S(2)}) copy-start(bf16[1,1,4096]{2,1,0:T(2,128)(2,1)} %param.14) | copy-start | bytes 24580
  227.9 82.5 %copy-start.4 = (f32[1,4096]{1,0:T(1,128)S(1)}, f32[1,4096]{1,0:T(1,128)}, u32[]{:S(2)}) copy-start(f32[1,4096]{1,0:T(1,128)} %param.24) | copy-start | bytes 49156
  240.5 184.1 %all-reduce.7.cloned.1.call-start = ((), (), s32[]{:S(2)}) async-start(), calls=%async_computation.6 | async-start | bytes 262144
  426.1 3.2 collective-permute-start
Sparse Core Ops, SparseCore 0:
  9.5 42.8 all-gather.6
  54.6 72.2 all-gather.8
  240.6 66.9 all-reduce.4
  355.6 68.9 all-reduce.6
where the time goes:
time: 437 us; the launch traced here: 436 us
  waiting for transfers between devices  262 us (60%)
  blocking collectives  73.1 us (17%)
  local copies, waits for them, and re-layouts  35.5 us (8%)
  matrix products  24.6 us (6%)
  other arithmetic  16.9 us (4%)
  between operations  14 us (3%)
  starting transfers between devices  10.4 us (2%)
    unnamed x6, waiting for transfers between devices  137 us
    all_gather x1, waiting for transfers between devices, shards(): lax.all_gather(tile_out[0], 'site', axis=0, tiled=True)  67.3 us
    all_to_all x1, waiting for transfers between devices, shards(): lax.all_to_all(encoded[send_index], 'site', split_axis=0, concat_axis=0,...  54.5 us
    all_gather x1, blocking collectives, shards(): everyone = lax.all_gather(current, 'site', axis=0, tiled=True)  32.7 us
    all_gather x1, blocking collectives, shards(): normed_rows = lax.all_gather(normed, 'site', axis=0, tiled=True)  30.5 us
    gather x1, local copies, waits for them, and re-layouts, shards(): encoded[send_index]  9.94 us
    all_to_all x1, blocking collectives, shards(): lax.all_to_all(combined, 'site', split_axis=1, concat_axis=0, tiled=True)  9.88 us
    dot_general x1, matrix products, shards(): jnp.dot(hidden, down_weight[0], preferred_element_type=jnp.float32)  9.34 us
  transfers between devices with their start and end apart: 7, of which 5 were waited for; matrix products, arithmetic and copies ran while one was open for 10% of the time, Pallas kernels for 0%

commit v1 on v0

--- a/solution.py
+++ b/solution.py
@@ -125,7 +125,12 @@
         tiled=True,
     )
     normed = rms_norm(residual, ffn_gain[0]).astype(jnp.bfloat16)
-    normed_rows = lax.all_gather(normed, "site", axis=0, tiled=True)
+    ring = [normed]
+    for hop in range(7):
+        ring.append(lax.ppermute(ring[-1], "site", [(dev, (dev + 1) % 8) for dev in range(8)]))
+    normed_rows = jnp.roll(
+        jnp.concatenate(ring[::-1], axis=0), (lax.axis_index("site") + 1) * ring[0].shape[0], axis=0
+    )
     gate_sum = by_rows(normed_rows, gate_weight[0])
     up_sum = by_rows(normed_rows, up_weight[0])
     hidden = (jax.nn.silu(gate_sum) * up_sum).astype(jnp.bfloat16)

time: 437 us -> 450 us (1.030)
  waiting for transfers between devices: 262 us -> 304 us
  blocking collectives: 73.1 us -> 42.6 us
    ppermute x0 -> x7, waiting for transfers between devices: none -> 44.4 us  [shards(): lax.ppermute(ring[-1], 'site', [(dev, (dev + 1) % 8) for dev in range(8)])]
    all_gather x1 -> x0, blocking collectives: 30.5 us -> none  [shards(): normed_rows = lax.all_gather(normed, 'site', axis=0, tiled=True)]
  transfers between devices with their start and end apart: 7 -> 14, of which waited for: 5 -> 12; matrix products, arithmetic and copies ran while one was open for 10% -> 10% of each run, Pallas kernels for 0% -> 0%
where the time goes in v1:
time: 450 us
  waiting for transfers between devices  304 us (68%)
  blocking collectives  42.6 us (9%)
  local copies, waits for them, and re-layouts  35.9 us (8%)
  matrix products  24.6 us (5%)
  other arithmetic  16.9 us (4%)
  between operations  14 us (3%)
  starting transfers between devices  11.2 us (2%)
    unnamed x6, waiting for transfers between devices  135 us
    all_gather x1, waiting for transfers between devices, shards(): lax.all_gather(tile_out[0], 'site', axis=0, tiled=True)  67.3 us
    all_to_all x1, waiting for transfers between devices, shards(): lax.all_to_all(encoded[send_index], 'site', split_axis=0, concat_axis=0,...  54.5 us
    ppermute x7, waiting for transfers between devices, shards(): lax.ppermute(ring[-1], 'site', [(dev, (dev + 1) % 8) for dev in range(8)])  44.4 us
    all_gather x1, blocking collectives, shards(): everyone = lax.all_gather(current, 'site', axis=0, tiled=True)  32.7 us
    gather x1, local copies, waits for them, and re-layouts, shards(): encoded[send_index]  9.94 us
    all_to_all x1, blocking collectives, shards(): lax.all_to_all(combined, 'site', split_axis=1, concat_axis=0, tiled=True)  9.88 us
    dot_general x1, matrix products, shards(): jnp.dot(hidden, down_weight[0], preferred_element_type=jnp.float32)  9.36 us
  transfers between devices with their start and end apart: 14, of which 12 were waited for; matrix products, arithmetic and copies ran while one was open for 10% of the time, Pallas kernels for 0%

profile of v1, /device:TPU:0, one launch (start us, length us, event | category | flops | bytes accessed | tf_op | source)
XLA Modules:
  0.0 449.5 jit_solution(5370801234495914777)
XLA Ops:
  6.6 0.7 all-gather.6.cloned.1.call-update
  7.3 0.7 all-gather.8.cloned.1.call-update
  8.0 32.7 %all-gather = bf16[8,1,4096]{2,1,0:T(2,128)(2,1)S(1)} all-gather(bf16[1,1,4096]{2,1,0:T(2,128)(2,1)} %param.14), channel_id=2, replica_groups=mesh['section'=4,'site'=8] {'site'}, dimensions={0}, use_global_device_ids=true | all-gather | bytes 73728 | tf_op jit(solution)/shard_map/all_gather | solution.py:106
  40.7 2.2 fusion.17
  43.0 0.6 broadcast.243
  43.6 0.6 reduce.9
  44.2 0.6 reshape.381
  44.8 5.4 %all-to-all-start = ((bf16[8,2,128]{2,1,0:T(2,128)(2,1)}), bf16[8,2,128]{2,1,0:T(2,128)(2,1)S(1)}, u32[]{:S(2)}, u32[]{:S(2)}) async-start(bf16[8,2,128]{2,1,0:T(2,128)(2,1)} %reshape.381), calls=%async_computation | async-start | bytes 8192 | tf_op jit(solution)/shard_map/all_to_all | solution.py:108
  51.3 8.0 %scatter_custom_fusion = s32[321]{0:T(512)S(1)} fusion(s32[2048]{0:T(1024)S(1)} %bitcast.149, s32[2048]{0:T(1024)S(1)} %bitcast.148, s32[]{:T(128)} %constant.104.clone.1), kind=kCustom, calls=%fused_computation.110 | custom fusion | bytes 1288 | tf_op jit(solution)/shard_map/scatter | solution.py:89
  59.6 67.3 %all-gather.8.cloned.1.call-done = bf16[1,512,4096]{2,1,0:T(8,128)(2,1)} async-done(((bf16[1,64,4096]{2,1,0:T(8,128)(2,1)}), bf16[1,512,4096]{2,1,0:T(8,128)(2,1)}) %all-gather.8.cloned.1.call-update) | async-done | bytes 4194320 | tf_op jit(solution)/shard_map/all_gather | solution.py:73
  126.9 6.1 %fusion.6 = f32[256,4096]{1,0:T(8,128)} fusion(bf16[1,512,4096]{2,1,0:T(8,128)(2,1)} %all-gather.8.cloned.1.call-done, bf16[1,1024,512]{2,1,0:T(8,128)(2,1)} %all-gather.6.cloned.1.call-done, bf16[1,256,1024]{2,1,0:T(8,128)(2,1)S(1)} %copy-done.1), kind=kOutput, calls=%fused_computation.9 | convolution fusion | flops 1343356928 | bytes 9961472 | tf_op jit(solution)/shard_map/dot_general | solution.py:41
  133.0 1.7 slice.54
  134.7 1.7 multiply_bitcast_fusion
  136.5 1.7 copy.36
  138.2 2.2 reduce_sum.46
  140.6 0.6 mul.170
  141.2 2.4 fusion.9
  143.6 1.5 pad_maximum_fusion
  145.1 9.9 %gather_fusion = bf16[320,4096]{1,0:T(8,128)(2,1)} fusion(bf16[256,4096]{1,0:T(8,128)(2,1)} %pad_maximum_fusion, s32[1024]{0:T(1024)S(1)} %pad_clamp_fusion.1), kind=kCustom, calls=%fused_computation | custom fusion | bytes 5244160 | tf_op jit(solution)/shard_map/gather | solution.py:103
  155.1 4.5 %all-to-all-start.1 = ((bf16[8,40,4096]{2,1,0:T(8,128)(2,1)}), bf16[8,40,4096]{2,1,0:T(8,128)(2,1)}, u32[]{:S(2)}, u32[]{:S(2)}) async-start(bf16[8,40,4096]{2,1,0:T(8,128)(2,1)} %bitcast.134), calls=%async_computation.1 | async-start | bytes 5242880 | tf_op jit(solution)/shard_map/all_to_all | solution.py:103
  159.8 0.6 dynamic_slice.10
  160.4 0.7 add_compare_fusion
  161.1 0.6 reduce-window.16
  162.0 0.7 iota_compare_fusion.3
  162.7 0.7 compare_select_fusion.2
  163.7 54.5 %all-to-all-done.1 = bf16[8,40,4096]{2,1,0:T(8,128)(2,1)} async-done(((bf16[8,40,4096]{2,1,0:T(8,128)(2,1)}), bf16[8,40,4096]{2,1,0:T(8,128)(2,1)}, u32[]{:S(2)}, u32[]{:S(2)}) %all-to-all-start.1) | async-done | bytes 2621472 | tf_op jit(solution)/shard_map/all_to_all | solution.py:103
  218.2 7.3 %gather_fusion.1 = bf16[256,4096]{1,0:T(8,128)(2,1)} fusion(bf16[320,4096]{1,0:T(8,128)(2,1)} %bitcast.16, s32[1024]{0:T(1024)S(1)} %pad_clamp_fusion), kind=kCustom, calls=%fused_computation.1 | custom fusion | bytes 4195328 | tf_op jit(solution)/shard_map/gather | solution.py:104
  225.5 2.1 copy.40
  228.9 0.7 reduce.10
  229.6 9.9 %all_to_all.31 = bf16[8,2,128]{2,1,0:T(2,128)(2,1)S(1)} all-to-all(bf16[8,2,128]{2,1,0:T(2,128)(2,1)S(1)} %reshape.383), channel_id=1, replica_groups=mesh['section'=4,'site'=8] {'site'}, dimensions={0} | all-to-all | bytes 8192 | tf_op jit(solution)/shard_map/all_to_all | solution.py:120
  239.4 1.0 fusion.10
  240.6 0.6 dynamic-slice
  241.2 66.5 %all-reduce.5.cloned.1.call-done = f32[8,4096]{1,0:T(8,128)} async-done(((f32[8,4096]{1,0:T(8,128)}), f32[8,4096]{1,0:T(8,128)}) %all-reduce.5.cloned.1.call-update) | async-done | bytes 131088
  307.6 2.2 multiply_reduce_fusion
  310.4 0.8 collective-permute-start
  311.3 5.7 %collective-permute-done = bf16[1,4096]{1,0:T(2,128)(2,1)S(1)} collective-permute-done((bf16[1,4096]{1,0:T(2,128)(2,1)S(1)}, bf16[1,4096]{1,0:T(2,128)(2,1)S(1)}, u32[]{:S(2)}, u32[]{:S(2)}) %collective-permute-start) | collective-permute-done | bytes 8224 | tf_op jit(solution)/shard_map/ppermute | solution.py:130
  316.9 6.4 %collective-permute-done.1 = bf16[1,4096]{1,0:T(2,128)(2,1)S(1)} collective-permute-done((bf16[1,4096]{1,0:T(2,128)(2,1)S(1)}, bf16[1,4096]{1,0:T(2,128)(2,1)S(1)}, u32[]{:S(2)}, u32[]{:S(2)}) %collective-permute-start.1) | collective-permute-done | bytes 8224 | tf_op jit(solution)/shard_map/ppermute | solution.py:130
  323.4 6.5 %collective-permute-done.2 = bf16[1,4096]{1,0:T(2,128)(2,1)S(1)} collective-permute-done((bf16[1,4096]{1,0:T(2,128)(2,1)S(1)}, bf16[1,4096]{1,0:T(2,128)(2,1)S(1)}, u32[]{:S(2)}, u32[]{:S(2)}) %collective-permute-start.2) | collective-permute-done | bytes 8224 | tf_op jit(solution)/shard_map/ppermute | solution.py:130
  329.9 6.4 %collective-permute-done.3 = bf16[1,4096]{1,0:T(2,128)(2,1)S(1)} collective-permute-done((bf16[1,4096]{1,0:T(2,128)(2,1)S(1)}, bf16[1,4096]{1,0:T(2,128)(2,1)S(1)}, u32[]{:S(2)}, u32[]{:S(2)}) %collective-permute-start.3) | collective-permute-done | bytes 8224 | tf_op jit(solution)/shard_map/ppermute | solution.py:130
  336.3 6.4 %collective-permute-done.4 = bf16[1,4096]{1,0:T(2,128)(2,1)S(1)} collective-permute-done((bf16[1,4096]{1,0:T(2,128)(2,1)S(1)}, bf16[1,4096]{1,0:T(2,128)(2,1)S(1)}, u32[]{:S(2)}, u32[]{:S(2)}) %collective-permute-start.4) | collective-permute-done | bytes 8224 | tf_op jit(solution)/shard_map/ppermute | solution.py:130
  342.8 6.4 %collective-permute-done.5 = bf16[1,4096]{1,0:T(2,128)(2,1)S(1)} collective-permute-done((bf16[1,4096]{1,0:T(2,128)(2,1)S(1)}, bf16[1,4096]{1,0:T(2,128)(2,1)S(1)}, u32[]{:S(2)}, u32[]{:S(2)}) %collective-permute-start.5) | collective-permute-done | bytes 8224 | tf_op jit(solution)/shard_map/ppermute | solution.py:130
  349.2 6.4 %collective-permute-done.6 = bf16[1,4096]{1,0:T(2,128)(2,1)S(1)} collective-permute-done((bf16[1,4096]{1,0:T(2,128)(2,1)S(1)}, bf16[1,4096]{1,0:T(2,128)(2,1)S(1)}, u32[]{:S(2)}, u32[]{:S(2)}) %collective-permute-start.6) | collective-permute-done | bytes 8224 | tf_op jit(solution)/shard_map/ppermute | solution.py:130
  356.0 5.1 %fusion.2 = f32[8,896]{1,0:T(8,128)S(1)} fusion(bf16[1,896,4096]{2,1,0:T(8,128)(2,1)} %param.26, bf16[16,4096]{1,0:T(8,128)(2,1)S(1)} %concatenate.11, s32[]{:T(128)S(6)} %select_n.88), kind=kOutput, calls=%fused_computation.5 | convolution fusion | flops 58720256 | bytes 7434244 | tf_op jit(solution)/shard_map/dot_general | solution.py:18
  361.1 9.4 %fusion = f32[8,4096]{1,0:T(8,128)} fusion(bf16[1,896,4096]{2,1,0:T(8,128)(2,1)} %param.27, f32[8,896]{1,0:T(8,128)S(1)} %fusion.2, bf16[1,896,4096]{2,1,0:T(8,128)(2,1)} %param.25, bf16[16,4096]{1,0:T(8,128)(2,1)S(1)} %concatenate.11, s32[]{:T(128)S(6)} %select_n.88), kind=kOutput, calls=%fused_computation.3 | convolution fusion | flops 117483520 | bytes 14905348 | tf_op jit(solution)/shard_map/dot_general | solution.py:140
  370.5 67.1 %all-reduce.7.cloned.1.call-done = f32[8,4096]{1,0:T(8,128)} async-done(((f32[8,4096]{1,0:T(8,128)}), f32[8,4096]{1,0:T(8,128)}) %all-reduce.7.cloned.1.call-update) | async-done | bytes 131088
  437.6 1.6 fusion.51
  439.2 3.2 collective-permute-done.7
  442.4 0.6 copy.69
  (77 shorter events, 4.2 us)
Async XLA Ops:
  6.5 232.9 %copy-start = (bf16[1,256,4096]{2,1,0:T(8,128)(2,1)S(1)}, bf16[1,256,4096]{2,1,0:T(8,128)(2,1)}, u32[]{:S(2)}) copy-start(bf16[1,256,4096]{2,1,0:T(8,128)(2,1)} %param.23) | copy-start | bytes 6291460
  6.5 43.7 %copy-start.3 = (s32[8,256]{1,0:T(8,128)S(1)}, s32[8,256]{1,0:T(8,128)}, u32[]{:S(2)}) copy-start(s32[8,256]{1,0:T(8,128)} %param.16) | copy-start | bytes 24580
  6.5 43.7 %copy-start.6 = (s32[8]{0:T(128)S(1)}, s32[8]{0:T(128)}, u32[]{:S(2)}) copy-start(s32[8]{0:T(128)} %param.17) | copy-start | bytes 100
  6.5 53.0 %copy-start.5 = (f32[1,128]{1,0:T(1,128)S(1)}, f32[1,128]{1,0:T(1,128)}, u32[]{:S(2)}) copy-start(f32[1,128]{1,0:T(1,128)} %param.20) | copy-start | bytes 1540
  6.5 120.3 %copy-start.1 = (bf16[1,256,1024]{2,1,0:T(8,128)(2,1)S(1)}, bf16[1,256,1024]{2,1,0:T(8,128)(2,1)}, u32[]{:S(2)}) copy-start(bf16[1,256,1024]{2,1,0:T(8,128)(2,1)} %param.15) | copy-start | bytes 1572868
  6.5 53.0 %all-gather.6.cloned.1.call-start = ((), (), s32[]{:S(2)}) async-start(), calls=%async_computation.3 | async-start | bytes 1179648 | tf_op jit(solution)/shard_map/all_gather | solution.py:72
  7.3 119.6 %all-gather.8.cloned.1.call-start = ((), (), s32[]{:S(2)}) async-start(), calls=%async_computation.4 | async-start | bytes 4718592 | tf_op jit(solution)/shard_map/all_gather | solution.py:73
  44.8 110.3 %all-to-all-start = ((bf16[8,2,128]{2,1,0:T(2,128)(2,1)}), bf16[8,2,128]{2,1,0:T(2,128)(2,1)S(1)}, u32[]{:S(2)}, u32[]{:S(2)}) async-start(bf16[8,2,128]{2,1,0:T(2,128)(2,1)} %reshape.381), calls=%async_computation | async-start | bytes 8192 | tf_op jit(solution)/shard_map/all_to_all | solution.py:108
  155.1 8.5 %copy-start.7 = (f32[1,128]{1,0:T(1,128)S(1)}, f32[1,128]{1,0:T(1,128)}, u32[]{:S(2)}) copy-start(f32[1,128]{1,0:T(1,128)} %param.19) | copy-start | bytes 1540
  155.1 63.1 %all-to-all-start.1 = ((bf16[8,40,4096]{2,1,0:T(8,128)(2,1)}), bf16[8,40,4096]{2,1,0:T(8,128)(2,1)}, u32[]{:S(2)}, u32[]{:S(2)}) async-start(bf16[8,40,4096]{2,1,0:T(8,128)(2,1)} %bitcast.134), calls=%async_computation.1 | async-start | bytes 5242880 | tf_op jit(solution)/shard_map/all_to_all | solution.py:103
  159.6 148.0 %all-reduce.5.cloned.1.call-start = ((), (), s32[]{:S(2)}) async-start(), calls=%async_computation.5 | async-start | bytes 262144
  227.9 12.7 %copy-start.8 = (u32[32]{0:T(128)S(1)}, u32[32]{0:T(128)}, u32[]{:S(2)}) copy-start(u32[32]{0:T(128)} %constant.133) | copy-start | bytes 388
  227.9 79.7 %copy-start.2 = (bf16[1,1,4096]{2,1,0:T(2,128)(2,1)S(1)}, bf16[1,1,4096]{2,1,0:T(2,128)(2,1)}, u32[]{:S(2)}) copy-start(bf16[1,1,4096]{2,1,0:T(2,128)(2,1)} %param.14) | copy-start | bytes 24580
  227.9 82.5 %copy-start.4 = (f32[1,4096]{1,0:T(1,128)S(1)}, f32[1,4096]{1,0:T(1,128)}, u32[]{:S(2)}) copy-start(f32[1,4096]{1,0:T(1,128)} %param.24) | copy-start | bytes 49156
  240.5 197.1 %all-reduce.7.cloned.1.call-start = ((), (), s32[]{:S(2)}) async-start(), calls=%async_computation.6 | async-start | bytes 262144
  310.4 6.5 %collective-permute-start = (bf16[1,4096]{1,0:T(2,128)(2,1)S(1)}, bf16[1,4096]{1,0:T(2,128)(2,1)S(1)}, u32[]{:S(2)}, u32[]{:S(2)}) collective-permute-start(bf16[1,4096]{1,0:T(2,128)(2,1)S(1)} %multiply_convert_fusion.1), channel_id=1, source_target_pairs={{0,1},{1,2},{2,3},{3,4},{4,5},{5,6},{6,7},{7,0},{8,9},{9,10},{10,1... | collective-permute-start | bytes 24584 | tf_op jit(solution)/shard_map/ppermute | solution.py:130
  316.9 6.4 %collective-permute-start.1 = (bf16[1,4096]{1,0:T(2,128)(2,1)S(1)}, bf16[1,4096]{1,0:T(2,128)(2,1)S(1)}, u32[]{:S(2)}, u32[]{:S(2)}) collective-permute-start(bf16[1,4096]{1,0:T(2,128)(2,1)S(1)} %collective-permute-done), channel_id=1, source_target_pairs={{0,1},{1,2},{2,3},{3,4},{4,5},{5,6},{6,7},{7,0},{8,9},{9,10},{10,1... | collective-permute-start | bytes 24584 | tf_op jit(solution)/shard_map/ppermute | solution.py:130
  323.4 6.5 %collective-permute-start.2 = (bf16[1,4096]{1,0:T(2,128)(2,1)S(1)}, bf16[1,4096]{1,0:T(2,128)(2,1)S(1)}, u32[]{:S(2)}, u32[]{:S(2)}) collective-permute-start(bf16[1,4096]{1,0:T(2,128)(2,1)S(1)} %collective-permute-done.1), channel_id=1, source_target_pairs={{0,1},{1,2},{2,3},{3,4},{4,5},{5,6},{6,7},{7,0},{8,9},{9,10},{10,1... | collective-permute-start | bytes 24584 | tf_op jit(solution)/shard_map/ppermute | solution.py:130
  329.9 6.4 %collective-permute-start.3 = (bf16[1,4096]{1,0:T(2,128)(2,1)S(1)}, bf16[1,4096]{1,0:T(2,128)(2,1)S(1)}, u32[]{:S(2)}, u32[]{:S(2)}) collective-permute-start(bf16[1,4096]{1,0:T(2,128)(2,1)S(1)} %collective-permute-done.2), channel_id=1, source_target_pairs={{0,1},{1,2},{2,3},{3,4},{4,5},{5,6},{6,7},{7,0},{8,9},{9,10},{10,1... | collective-permute-start | bytes 24584 | tf_op jit(solution)/shard_map/ppermute | solution.py:130
  336.3 6.4 %collective-permute-start.4 = (bf16[1,4096]{1,0:T(2,128)(2,1)S(1)}, bf16[1,4096]{1,0:T(2,128)(2,1)S(1)}, u32[]{:S(2)}, u32[]{:S(2)}) collective-permute-start(bf16[1,4096]{1,0:T(2,128)(2,1)S(1)} %collective-permute-done.3), channel_id=1, source_target_pairs={{0,1},{1,2},{2,3},{3,4},{4,5},{5,6},{6,7},{7,0},{8,9},{9,10},{10,1... | collective-permute-start | bytes 24584 | tf_op jit(solution)/shard_map/ppermute | solution.py:130
  342.8 6.4 %collective-permute-start.5 = (bf16[1,4096]{1,0:T(2,128)(2,1)S(1)}, bf16[1,4096]{1,0:T(2,128)(2,1)S(1)}, u32[]{:S(2)}, u32[]{:S(2)}) collective-permute-start(bf16[1,4096]{1,0:T(2,128)(2,1)S(1)} %collective-permute-done.4), channel_id=1, source_target_pairs={{0,1},{1,2},{2,3},{3,4},{4,5},{5,6},{6,7},{7,0},{8,9},{9,10},{10,1... | collective-permute-start | bytes 24584 | tf_op jit(solution)/shard_map/ppermute | solution.py:130
  349.2 6.4 %collective-permute-start.6 = (bf16[1,4096]{1,0:T(2,128)(2,1)S(1)}, bf16[1,4096]{1,0:T(2,128)(2,1)S(1)}, u32[]{:S(2)}, u32[]{:S(2)}) collective-permute-start(bf16[1,4096]{1,0:T(2,128)(2,1)S(1)} %collective-permute-done.5), channel_id=1, source_target_pairs={{0,1},{1,2},{2,3},{3,4},{4,5},{5,6},{6,7},{7,0},{8,9},{9,10},{10,1... | collective-permute-start | bytes 24584 | tf_op jit(solution)/shard_map/ppermute | solution.py:130
  439.2 3.2 collective-permute-start.7
Sparse Core Ops, SparseCore 0:
  9.5 42.8 all-gather.5
  54.6 72.2 all-gather.7
  240.6 66.9 all-reduce.4
  370.6 66.9 all-reduce.6
